TPU v7x, 512 devices: a whole 4x4x16 slice. The times are simulated.
512 devices in a mesh: grp: 16 (over z_hi, x, core), dev: 32 (over y, z_lo).
Axes of the slice: x: 4, y: 4, z: 16 (z_hi: 2, z_lo: 8; z = z_hi * 8 + z_lo), core: 2. Of those that a mesh axis runs over, the one named last changes fastest.
Arguments:
- samples: bfloat16 [16384, 1024], P(('grp', 'dev')), may hold values from -0.1875 to 0.1875
- set_labels: int32 [16384], P(('grp', 'dev')), may hold values 0 or 1
- sign_words: int32 [16384, 25], P(('grp', 'dev')), may hold values from 0 to 2097151
- corpus: bfloat16 [16384, 1024], P(('grp', 'dev')), may hold values from -0.1875 to 0.1875
- scale_grid: float32 [16], replicated, may hold values from 0.25 to 4
- scale_pick: int32 [4], replicated, may hold values from 0 to 15
Outputs:
- quad_forms: float32 [4, 512], replicated
- test_scores: float32 [4], replicated
- proof: float32 [4, 16384], P(None, ('grp', 'dev'))
Inputs may be any that keep to these rules, and one draw needn't show every extreme that they name: `sign_words`: every word is below 2 ** 21; each of its 21 bits is a sign, 1 for +1 and 0 for -1. `scale_pick`: indices into the grid, from 0 to 15.
All inputs are finite; a program needn't handle non-finite values. No bound on the sum of `set_labels` on one device may be relied on, other than what follows from the above.
Results may differ from a plain program's by a relative error of at most 0.0099.
Values may be sent and summed in bfloat16 or wider, within the bound.
No kernel may reach another device: no remote copies, remote signals or barrier semaphores. Data moves between devices by JAX's collectives and lax.ppermute only.
A program may use at most 64 MiB of HBM per device.

v0:
```python
import numpy as np
import jax
import jax.numpy as jnp
from jax import lax
from jax.sharding import PartitionSpec as P

NB = 4
BOOT = 511
D = 1024
META = 128
CHUNK = 7
word_bits = 21


def make_vectors(set_labels, sign_words):
    weights = (1 - 2 * set_labels).astype(jnp.float32)
    shifts = jnp.arange(word_bits, dtype=jnp.int32)
    bit_flags = jnp.right_shift(sign_words[:, :, None], shifts[None, None, :]) & 1
    bit_flags = bit_flags.reshape(sign_words.shape[0], -1)[:, :BOOT]
    sign_values = (2 * bit_flags - 1).astype(jnp.float32)
    vectors = jnp.concatenate([weights[:, None], sign_values * weights[:, None]], axis=1)
    return vectors.astype(jnp.bfloat16)


def band_scales(scale_grid, scale_pick):
    onehot = (
        scale_pick[:, None] == jnp.arange(scale_grid.shape[0], dtype=jnp.int32)[None, :]
    ).astype(jnp.float32)
    chosen = jnp.sum(onehot * scale_grid[None, :], axis=1)
    return 0.5 / chosen


def squares(matrix):
    wide = matrix.astype(jnp.float32)
    return jnp.sum(wide * wide, axis=1)


def distances(left, left_sq, right, right_sq):
    cross = lax.dot_general(
        left, right, (((1,), (1,)), ((), ())), preferred_element_type=jnp.float32
    )
    return left_sq[:, None] + right_sq[None, :] - 2.0 * cross


def pack_meta(set_labels, sign_words):
    words = sign_words.shape[1]
    chunks = [sign_words >> CHUNK * c & (1 << CHUNK) - 1 for c in range(3)]
    meta = jnp.concatenate([set_labels[:, None]] + chunks, axis=1)
    pad = META - meta.shape[1]
    meta = jnp.pad(meta, ((0, 0), (0, pad)))
    return (meta.astype(jnp.bfloat16), words)


def unpack(buf, words):
    rows = buf[:, :D]
    meta = buf[:, D : D + 1 + 3 * words].astype(jnp.float32).astype(jnp.int32)
    labels = meta[:, 0]
    c = [meta[:, 1 + k * words : 1 + (k + 1) * words] for k in range(3)]
    sign_words = c[0] + (c[1] << CHUNK) + (c[2] << 2 * CHUNK)
    return (rows, make_vectors(labels, sign_words))


def xor_gather(x, axis, n, bits):
    idx = lax.axis_index(axis)
    buf = x[None]
    for b in bits:
        k = 1 << b
        other = lax.ppermute(buf, axis, [(i, i ^ k) for i in range(n)])
        lo = idx & k == 0
        buf = jnp.where(lo, jnp.concatenate([buf, other]), jnp.concatenate([other, buf]))
    order = [sum(((t >> j & 1) << b for j, b in enumerate(bits))) for t in range(n)]
    return (buf, order)


def per_device(samples, set_labels, sign_words, corpus, scale_grid, scale_pick):
    scales = band_scales(scale_grid, scale_pick)
    n_grp = lax.axis_size("grp")
    n_dev = lax.axis_size("dev")
    rows_here = samples.shape[0]
    total = rows_here * n_grp * n_dev
    inv_root = jnp.float32(1.0) / jnp.sqrt(jnp.float32(total))
    meta, words = pack_meta(set_labels, sign_words)
    own = jnp.concatenate([samples, meta], axis=1)
    own_wide = jnp.concatenate([own, corpus], axis=1)
    grp_bits = [b for b in range(1, n_grp.bit_length() - 1)] + [0]
    dev_bits = list(range(n_dev.bit_length() - 1))
    col_buf, col_order = xor_gather(own_wide, "grp", n_grp, grp_bits)
    blk_buf, _ = xor_gather(own, "dev", n_dev, dev_bits)
    col_buf = col_buf.reshape(n_grp * rows_here, -1)
    blk_buf = blk_buf.reshape(n_dev * rows_here, -1)
    col_rows, col_vec = unpack(col_buf[:, : D + META], words)
    col_corpus = col_buf[:, D + META :]
    block_rows, block_vec = unpack(blk_buf, words)
    col_sq = squares(col_rows)
    block_sq = squares(block_rows)
    dist = distances(block_rows, block_sq, col_rows, col_sq)
    block_wide = block_vec.astype(jnp.float32)
    forms = []
    for kernel_id in range(NB):
        kern = jnp.exp(-dist * scales[kernel_id]).astype(jnp.bfloat16)
        product = jnp.dot(kern, col_vec, preferred_element_type=jnp.float32)
        forms.append(jnp.sum(block_wide * product, axis=0))
    forms_part = jnp.stack(forms)
    cdist = distances(col_corpus, squares(col_corpus), block_rows, block_sq)
    weights = block_vec[:, 0]
    proofs = []
    for kernel_id in range(NB):
        kern = jnp.exp(-cdist * scales[kernel_id]).astype(jnp.bfloat16)
        proofs.append(jnp.dot(kern, weights, preferred_element_type=jnp.float32))
    proof_part = jnp.stack(proofs).reshape(NB, n_grp, rows_here)
    inverse = np.argsort(np.array(col_order))
    proof_part = jnp.take(proof_part, jnp.asarray(inverse, jnp.int32), axis=1)
    proof_part = jnp.transpose(proof_part, (1, 0, 2))
    got = lax.all_to_all(proof_part, "grp", 0, 0, tiled=True)
    proof = jnp.sum(got, axis=0) * inv_root
    quad_forms = lax.psum(forms_part, ("grp", "dev")) / total
    bootstrap = quad_forms[:, 1:]
    centre = jnp.mean(bootstrap, axis=1)
    spread = jnp.mean(jnp.square(bootstrap - centre[:, None]), axis=1)
    test_scores = (quad_forms[:, 0] - centre) / jnp.sqrt(spread + 1e-06)
    return (quad_forms, test_scores, proof)


def solution(mesh):
    in_specs = (
        P(("grp", "dev"), None),
        P(("grp", "dev")),
        P(("grp", "dev"), None),
        P(("grp", "dev"), None),
        P(),
        P(),
    )
    out_specs = (P(), P(), P(None, ("grp", "dev")))
    return jax.shard_map(
        per_device, mesh=mesh, in_specs=in_specs, out_specs=out_specs, check_vma=False
    )
```

profile of v0, /device:TPU:1, one launch (start us, length us, event | category | flops | bytes accessed | tf_op | source)
XLA Modules:
  0.0 325.1 jit_solution(3288057333134248958)
XLA Ops:
  0.6 0.7 and_convert_fusion.2
  1.4 0.7 convert_bitcast_fusion
  2.2 0.9 maximum_bitcast_fusion
  3.1 3.9 %collective-permute-start.5 = (bf16[1,32,2176]{2,1,0:T(8,128)(2,1)S(1)}, bf16[1,32,2176]{2,1,0:T(8,128)(2,1)S(1)}, u32[]{:S(2)}, u32[]{:S(2)}) collective-permute-start(bf16[1,32,2176]{2,1,0:T(8,128)(2,1)S(1)} %maximum_bitcast_fusion), channel_id=1, source_target_pairs={{0,64},{32,96},{64,0},{96,32},{128,192},{160,224},{192,128},{224,1... | collective-permute-start | bytes 417800 | tf_op jit(solution)/shard_map/ppermute | solution.py:68
  7.1 2.4 collective-permute-done.5
  9.5 5.5 %collective-permute-start.6 = (bf16[2,32,2176]{2,1,0:T(8,128)(2,1)S(1)}, bf16[2,32,2176]{2,1,0:T(8,128)(2,1)S(1)}, u32[]{:S(2)}, u32[]{:S(2)}) collective-permute-start(bf16[2,32,2176]{2,1,0:T(8,128)(2,1)S(1)} %maximum_select_fusion.7), channel_id=1, source_target_pairs={{0,128},{32,160},{64,192},{96,224},{128,0},{160,32},{192,64},{224,... | collective-permute-start | bytes 835592 | tf_op jit(solution)/shard_map/ppermute | solution.py:68
  15.1 0.8 maximum_bitcast_fusion.1
  15.9 3.5 %collective-permute-start = (bf16[1,32,1152]{2,1,0:T(8,128)(2,1)S(1)}, bf16[1,32,1152]{2,1,0:T(8,128)(2,1)S(1)}, u32[]{:S(2)}, u32[]{:S(2)}) collective-permute-start(bf16[1,32,1152]{2,1,0:T(8,128)(2,1)S(1)} %maximum_bitcast_fusion.1), channel_id=1, source_target_pairs={{0,1},{1,0},{2,3},{3,2},{4,5},{5,4},{6,7},{7,6},{8,9},{9,8},{10,11... | collective-permute-start | bytes 221192 | tf_op jit(solution)/shard_map/ppermute | solution.py:68
  19.6 16.4 %collective-permute-start.7 = (bf16[4,32,2176]{2,1,0:T(8,128)(2,1)S(1)}, bf16[4,32,2176]{2,1,0:T(8,128)(2,1)S(1)}, u32[]{:S(2)}, u32[]{:S(2)}) collective-permute-start(bf16[4,32,2176]{2,1,0:T(8,128)(2,1)S(1)} %maximum_select_fusion.5), channel_id=1, source_target_pairs={{0,256},{32,288},{64,320},{96,352},{128,384},{160,416},{192,448},{... | collective-permute-start | bytes 1671176 | tf_op jit(solution)/shard_map/ppermute | solution.py:68
  36.1 3.2 collective-permute-start.1
  39.4 52.6 %collective-permute-done.1 = bf16[2,32,1152]{2,1,0:T(8,128)(2,1)S(1)} collective-permute-done((bf16[2,32,1152]{2,1,0:T(8,128)(2,1)S(1)}, bf16[2,32,1152]{2,1,0:T(8,128)(2,1)S(1)}, u32[]{:S(2)}, u32[]{:S(2)}) %collective-permute-start.1) | collective-permute-done | bytes 147488 | tf_op jit(solution)/shard_map/ppermute | solution.py:68
  92.1 2.0 collective-permute-start.2
  94.3 2.7 collective-permute-start.8
  97.0 26.5 %collective-permute-done.2 = bf16[4,32,1152]{2,1,0:T(8,128)(2,1)S(1)} collective-permute-done((bf16[4,32,1152]{2,1,0:T(8,128)(2,1)S(1)}, bf16[4,32,1152]{2,1,0:T(8,128)(2,1)S(1)}, u32[]{:S(2)}, u32[]{:S(2)}) %collective-permute-start.2) | collective-permute-done | bytes 294944 | tf_op jit(solution)/shard_map/ppermute | solution.py:68
  123.6 3.2 collective-permute-start.3
  127.2 0.7 fusion.55
  127.8 12.1 %collective-permute-done.3 = bf16[8,32,1152]{2,1,0:T(8,128)(2,1)S(1)} collective-permute-done((bf16[8,32,1152]{2,1,0:T(8,128)(2,1)S(1)}, bf16[8,32,1152]{2,1,0:T(8,128)(2,1)S(1)}, u32[]{:S(2)}, u32[]{:S(2)}) %collective-permute-start.3) | collective-permute-done | bytes 589856 | tf_op jit(solution)/shard_map/ppermute | solution.py:68
  139.9 1.2 maximum_select_fusion.2
  141.1 4.8 %collective-permute-start.4 = (bf16[16,32,1152]{2,1,0:T(8,128)(2,1)}, bf16[16,32,1152]{2,1,0:T(8,128)(2,1)}, u32[]{:S(2)}, u32[]{:S(2)}) collective-permute-start(bf16[16,32,1152]{2,1,0:T(8,128)(2,1)} %maximum_select_fusion.2), channel_id=1, source_target_pairs={{0,16},{1,17},{2,18},{3,19},{4,20},{5,21},{6,22},{7,23},{8,24},{9,... | collective-permute-start | bytes 3538952 | tf_op jit(solution)/shard_map/ppermute | solution.py:68
  145.9 2.0 maximum_select_fusion.1
  148.0 0.9 convert_convert_fusion.1
  148.9 1.0 fusion.26
  150.1 1.2 shift_right_arithmetic.71
  151.2 0.8 fusion.53
  152.8 18.2 %collective-permute-done.4 = bf16[16,32,1152]{2,1,0:T(8,128)(2,1)} collective-permute-done((bf16[16,32,1152]{2,1,0:T(8,128)(2,1)}, bf16[16,32,1152]{2,1,0:T(8,128)(2,1)}, u32[]{:S(2)}, u32[]{:S(2)}) %collective-permute-start.4) | collective-permute-done | bytes 1179680 | tf_op jit(solution)/shard_map/ppermute | solution.py:68
  171.0 2.6 maximum_select_fusion
  174.1 0.9 copy-done
  175.6 1.7 shift_right_arithmetic.65
  177.3 2.2 fusion.9
  179.6 2.5 subtract_negate_fusion.1
  182.1 1.6 fusion
  183.7 1.6 fusion.1
  185.4 1.6 fusion.2
  186.9 1.6 fusion.3
  188.5 102.5 %psum.7 = f32[4,512]{1,0:T(4,128)S(1)} all-reduce(f32[4,512]{1,0:T(4,128)S(1)} %pad_maximum_fusion.3), channel_id=1, replica_groups=mesh['grp'=16,'dev'=32] {'grp','dev'}, use_global_device_ids=true, to_apply=%region_7.8 | all-reduce | flops 2048 | bytes 16384 | tf_op jit(solution)/shard_map/psum | solution.py:116
  291.4 6.0 %exponential_convert_fusion.3 = (bf16[512,1024]{1,0:T(8,128)(2,1)S(1)}, bf16[512,1024]{1,0:T(8,128)(2,1)S(1)}, bf16[512,1024]{1,0:T(8,128)(2,1)S(1)}, bf16[512,1024]{1,0:T(8,128)(2,1)S(1)}) fusion(f32[]{:T(128)} %bitcast.6, f32[]{:T(128)} %bitcast.13, f32[]{:T(128)} %bitcast.11, f32[]{:T(128)} %bitcast.9, bf16[1024,1152]{1,0:T(8,128)(2,1)S(1)} %bitcast.50, ...), kind=kOutput, calls=%fused_computation.22 | convolution fusion | flops 1080033280 | bytes 7348224 | tf_op jit(solution)/shard_map/dot_general | solution.py:39
  297.4 0.8 fusion.43
  298.1 0.8 fusion.41
  298.9 0.8 fusion.39
  299.7 0.8 fusion.37
  300.6 0.6 gather_fusion
  301.2 0.7 reshape.96
  301.8 7.2 %all-to-all-start = ((f32[16,1,128]{2,1,0:T(1,128)}), f32[16,1,128]{2,1,0:T(1,128)S(1)}, u32[]{:S(2)}, u32[]{:S(2)}) async-start(f32[16,1,128]{2,1,0:T(1,128)} %reshape.96), calls=%async_computation | async-start | bytes 16384 | tf_op jit(solution)/shard_map/all_to_all | solution.py:114
  309.2 0.5 rsqrt_multiply_fusion
  309.8 13.5 %all-to-all-done = f32[16,1,128]{2,1,0:T(1,128)S(1)} async-done(((f32[16,1,128]{2,1,0:T(1,128)}), f32[16,1,128]{2,1,0:T(1,128)S(1)}, u32[]{:S(2)}, u32[]{:S(2)}) %all-to-all-start) | async-done | bytes 8224 | tf_op jit(solution)/shard_map/all_to_all | solution.py:114
  323.3 0.5 broadcast.108
  323.8 0.7 reduce.2
  324.6 0.6 broadcast_multiply_fusion.1
  (54 shorter events, 3.8 us)
Async XLA Ops:
  3.1 6.4 %collective-permute-start.5 = (bf16[1,32,2176]{2,1,0:T(8,128)(2,1)S(1)}, bf16[1,32,2176]{2,1,0:T(8,128)(2,1)S(1)}, u32[]{:S(2)}, u32[]{:S(2)}) collective-permute-start(bf16[1,32,2176]{2,1,0:T(8,128)(2,1)S(1)} %maximum_bitcast_fusion), channel_id=1, source_target_pairs={{0,64},{32,96},{64,0},{96,32},{128,192},{160,224},{192,128},{224,1... | collective-permute-start | bytes 417800 | tf_op jit(solution)/shard_map/ppermute | solution.py:68
  9.5 10.0 %collective-permute-start.6 = (bf16[2,32,2176]{2,1,0:T(8,128)(2,1)S(1)}, bf16[2,32,2176]{2,1,0:T(8,128)(2,1)S(1)}, u32[]{:S(2)}, u32[]{:S(2)}) collective-permute-start(bf16[2,32,2176]{2,1,0:T(8,128)(2,1)S(1)} %maximum_select_fusion.7), channel_id=1, source_target_pairs={{0,128},{32,160},{64,192},{96,224},{128,0},{160,32},{192,64},{224,... | collective-permute-start | bytes 835592 | tf_op jit(solution)/shard_map/ppermute | solution.py:68
  15.9 20.1 %collective-permute-start = (bf16[1,32,1152]{2,1,0:T(8,128)(2,1)S(1)}, bf16[1,32,1152]{2,1,0:T(8,128)(2,1)S(1)}, u32[]{:S(2)}, u32[]{:S(2)}) collective-permute-start(bf16[1,32,1152]{2,1,0:T(8,128)(2,1)S(1)} %maximum_bitcast_fusion.1), channel_id=1, source_target_pairs={{0,1},{1,0},{2,3},{3,2},{4,5},{5,4},{6,7},{7,6},{8,9},{9,8},{10,11... | collective-permute-start | bytes 221192 | tf_op jit(solution)/shard_map/ppermute | solution.py:68
  19.6 74.5 %collective-permute-start.7 = (bf16[4,32,2176]{2,1,0:T(8,128)(2,1)S(1)}, bf16[4,32,2176]{2,1,0:T(8,128)(2,1)S(1)}, u32[]{:S(2)}, u32[]{:S(2)}) collective-permute-start(bf16[4,32,2176]{2,1,0:T(8,128)(2,1)S(1)} %maximum_select_fusion.5), channel_id=1, source_target_pairs={{0,256},{32,288},{64,320},{96,352},{128,384},{160,416},{192,448},{... | collective-permute-start | bytes 1671176 | tf_op jit(solution)/shard_map/ppermute | solution.py:68
  36.1 90.8 %copy-start.5 = (s32[16]{0:T(128)S(1)}, s32[16]{0:T(128)}, u32[]{:S(2)}) copy-start(s32[16]{0:T(128)} %constant.97) | copy-start | bytes 196
  36.1 90.8 %copy-start.6 = (f32[16]{0:T(128)S(1)}, f32[16]{0:T(128)}, u32[]{:S(2)}) copy-start(f32[16]{0:T(128)} %param.11) | copy-start | bytes 196
  36.1 90.8 %copy-start.7 = (s32[4]{0:T(128)S(1)}, s32[4]{0:T(128)}, u32[]{:S(2)}) copy-start(s32[4]{0:T(128)} %param.12) | copy-start | bytes 52
  36.1 55.9 %collective-permute-start.1 = (bf16[2,32,1152]{2,1,0:T(8,128)(2,1)S(1)}, bf16[2,32,1152]{2,1,0:T(8,128)(2,1)S(1)}, u32[]{:S(2)}, u32[]{:S(2)}) collective-permute-start(bf16[2,32,1152]{2,1,0:T(8,128)(2,1)S(1)} %maximum_select_fusion.8), channel_id=1, source_target_pairs={{0,2},{1,3},{2,0},{3,1},{4,6},{5,7},{6,4},{7,5},{8,10},{9,11},{10,... | collective-permute-start | bytes 442376 | tf_op jit(solution)/shard_map/ppermute | solution.py:68
  92.1 31.4 %collective-permute-start.2 = (bf16[4,32,1152]{2,1,0:T(8,128)(2,1)S(1)}, bf16[4,32,1152]{2,1,0:T(8,128)(2,1)S(1)}, u32[]{:S(2)}, u32[]{:S(2)}) collective-permute-start(bf16[4,32,1152]{2,1,0:T(8,128)(2,1)S(1)} %maximum_select_fusion.6), channel_id=1, source_target_pairs={{0,4},{1,5},{2,6},{3,7},{4,0},{5,1},{6,2},{7,3},{8,12},{9,13},{10,... | collective-permute-start | bytes 884744 | tf_op jit(solution)/shard_map/ppermute | solution.py:68
  94.3 51.6 %collective-permute-start.8 = (bf16[8,32,2176]{2,1,0:T(8,128)(2,1)S(1)}, bf16[8,32,2176]{2,1,0:T(8,128)(2,1)}, u32[]{:S(2)}, u32[]{:S(2)}) collective-permute-start(bf16[8,32,2176]{2,1,0:T(8,128)(2,1)S(1)} %maximum_select_fusion.3), channel_id=1, source_target_pairs={{0,32},{32,0},{64,96},{96,64},{128,160},{160,128},{192,224},{224,1... | collective-permute-start | bytes 3342344 | tf_op jit(solution)/shard_map/ppermute | solution.py:68
  123.6 16.3 %collective-permute-start.3 = (bf16[8,32,1152]{2,1,0:T(8,128)(2,1)S(1)}, bf16[8,32,1152]{2,1,0:T(8,128)(2,1)S(1)}, u32[]{:S(2)}, u32[]{:S(2)}) collective-permute-start(bf16[8,32,1152]{2,1,0:T(8,128)(2,1)S(1)} %maximum_select_fusion.4), channel_id=1, source_target_pairs={{0,8},{1,9},{2,10},{3,11},{4,12},{5,13},{6,14},{7,15},{8,0},{9,1},... | collective-permute-start | bytes 1769480 | tf_op jit(solution)/shard_map/ppermute | solution.py:68
  141.1 29.9 %collective-permute-start.4 = (bf16[16,32,1152]{2,1,0:T(8,128)(2,1)}, bf16[16,32,1152]{2,1,0:T(8,128)(2,1)}, u32[]{:S(2)}, u32[]{:S(2)}) collective-permute-start(bf16[16,32,1152]{2,1,0:T(8,128)(2,1)} %maximum_select_fusion.2), channel_id=1, source_target_pairs={{0,16},{1,17},{2,18},{3,19},{4,20},{5,21},{6,22},{7,23},{8,24},{9,... | collective-permute-start | bytes 3538952 | tf_op jit(solution)/shard_map/ppermute | solution.py:68
  147.9 4.1 %copy-start.2 = (bf16[16,32,2176]{2,1,0:T(8,128)(2,1)}, bf16[16,32,2176]{2,1,0:T(8,128)(2,1)S(1)}, u32[]{:S(2)}) copy-start(bf16[16,32,2176]{2,1,0:T(8,128)(2,1)S(1)} %maximum_select_fusion.1) | copy-start | bytes 6684676
  151.2 1.3 copy-start.3
  173.6 1.4 copy-start
  177.3 2.3 copy-start.1
  291.1 18.0 %copy-start.4 = (f32[4,512]{1,0:T(4,128)}, f32[4,512]{1,0:T(4,128)S(1)}, u32[]{:S(2)}) copy-start(f32[4,512]{1,0:T(4,128)S(1)} %broadcast_multiply_fusion) | copy-start | bytes 24580
  301.8 21.4 %all-to-all-start = ((f32[16,1,128]{2,1,0:T(1,128)}), f32[16,1,128]{2,1,0:T(1,128)S(1)}, u32[]{:S(2)}, u32[]{:S(2)}) async-start(f32[16,1,128]{2,1,0:T(1,128)} %reshape.96), calls=%async_computation | async-start | bytes 16384 | tf_op jit(solution)/shard_map/all_to_all | solution.py:114
where the time goes:
time: 326 us; the launch traced here: 325 us
  waiting for transfers between devices  125 us (38%)
  blocking collectives  103 us (32%)
  starting transfers between devices  52.6 us (16%)
  other arithmetic  18.2 us (6%)
  matrix products  18.1 us (6%)
  local copies, waits for them, and re-layouts  7.41 us (2%)
    ppermute x9, waiting for transfers between devices, xor_gather(): other = lax.ppermute(buf, axis, [(i, i ^ k) for i in range(n)])  112 us
    psum x1, blocking collectives, per_device(): quad_forms = lax.psum(forms_part, ('grp', 'dev')) / total  103 us
    ppermute x9, starting transfers between devices, xor_gather(): other = lax.ppermute(buf, axis, [(i, i ^ k) for i in range(n)])  45.4 us
    all_to_all x1, waiting for transfers between devices, per_device(): got = lax.all_to_all(proof_part, 'grp', 0, 0, tiled=True)  13.5 us
    dot_general x2, matrix products, distances(): lax.dot_general(left, right, (((1,), (1,)), ((), ())), preferred_element_...  8.49 us
    all_to_all x1, starting transfers between devices, per_device(): got = lax.all_to_all(proof_part, 'grp', 0, 0, tiled=True)  7.18 us
  transfers between devices with their start and end apart: 10, of which 6 were waited for; matrix products, arithmetic and copies ran while one was open for 3% of the time, Pallas kernels for 0%

commit v1 on v0

--- a/solution.py
+++ b/solution.py
@@ -113,7 +113,7 @@
     proof_part = jnp.transpose(proof_part, (1, 0, 2))
     got = lax.all_to_all(proof_part, "grp", 0, 0, tiled=True)
     proof = jnp.sum(got, axis=0) * inv_root
-    quad_forms = lax.psum(forms_part, ("grp", "dev")) / total
+    quad_forms = jnp.sum(lax.all_gather(forms_part, ("grp", "dev")), axis=0) / total
     bootstrap = quad_forms[:, 1:]
     centre = jnp.mean(bootstrap, axis=1)
     spread = jnp.mean(jnp.square(bootstrap - centre[:, None]), axis=1)

time: 326 us -> 1640 us (5.03)
  waiting for transfers between devices: 125 us -> 1500 us
  blocking collectives: 103 us -> 22.1 us
    all_gather x0 -> x1, waiting for transfers between devices: none -> 1390 us  [per_device(): lax.all_gather(forms_part, ('grp', 'dev'))]
    psum x1 -> x0, blocking collectives: 103 us -> none  [per_device(): quad_forms = lax.psum(forms_part, ('grp', 'dev')) / total]
    all_to_all x0 -> x1, blocking collectives: none -> 22.1 us  [per_device(): got = lax.all_to_all(proof_part, 'grp', 0, 0, tiled=True)]
  transfers between devices with their start and end apart: 10 -> 10, of which waited for: 6 -> 6; matrix products, arithmetic and copies ran while one was open for 3% -> 1% of each run, Pallas kernels for 0% -> 0%
where the time goes in v1:
time: 1640 us; the launch traced here: 1630 us
  waiting for transfers between devices  1500 us (91%)
  starting transfers between devices  45.3 us (3%)
  blocking collectives  22.1 us (1%)
  other arithmetic  21.7 us (1%)
  matrix products  18.1 us (1%)
    all_gather x1, waiting for transfers between devices, per_device(): lax.all_gather(forms_part, ('grp', 'dev'))  1390 us
    ppermute x9, waiting for transfers between devices, xor_gather(): other = lax.ppermute(buf, axis, [(i, i ^ k) for i in range(n)])  112 us
    ppermute x9, starting transfers between devices, xor_gather(): other = lax.ppermute(buf, axis, [(i, i ^ k) for i in range(n)])  45.3 us
  transfers between devices with their start and end apart: 10, of which 6 were waited for; matrix products, arithmetic and copies ran while one was open for 1% of the time, Pallas kernels for 0%

profile of v1, /device:TPU:1, one launch (start us, length us, event | category | flops | bytes accessed | tf_op | source)
XLA Modules:
  0.0 1631.3 jit_solution(5167243469616031819)
XLA Ops:
  7.2 0.7 and_convert_fusion.2
  7.9 0.7 convert_bitcast_fusion
  8.8 0.9 maximum_bitcast_fusion
  9.7 3.9 collective-permute-start.5
  13.6 2.4 collective-permute-done.5
  16.1 5.5 collective-permute-start.6
  21.6 0.8 maximum_bitcast_fusion.1
  22.5 3.5 collective-permute-start
  26.2 16.4 %collective-permute-start.7 = (bf16[4,32,2176]{2,1,0:T(8,128)(2,1)S(1)}, bf16[4,32,2176]{2,1,0:T(8,128)(2,1)S(1)}, u32[]{:S(2)}, u32[]{:S(2)}) collective-permute-start(bf16[4,32,2176]{2,1,0:T(8,128)(2,1)S(1)} %maximum_select_fusion.5), channel_id=1, source_target_pairs={{0,256},{32,288},{64,320},{96,352},{128,384},{160,416},{192,448},{... | collective-permute-start | bytes 1671176 | tf_op jit(solution)/shard_map/ppermute | solution.py:68
  42.7 3.1 collective-permute-start.1
  45.8 52.8 %collective-permute-done.1 = bf16[2,32,1152]{2,1,0:T(8,128)(2,1)S(1)} collective-permute-done((bf16[2,32,1152]{2,1,0:T(8,128)(2,1)S(1)}, bf16[2,32,1152]{2,1,0:T(8,128)(2,1)S(1)}, u32[]{:S(2)}, u32[]{:S(2)}) %collective-permute-start.1) | collective-permute-done | bytes 147488 | tf_op jit(solution)/shard_map/ppermute | solution.py:68
  98.6 2.0 collective-permute-start.2
  100.9 2.7 collective-permute-start.8
  103.6 26.5 %collective-permute-done.2 = bf16[4,32,1152]{2,1,0:T(8,128)(2,1)S(1)} collective-permute-done((bf16[4,32,1152]{2,1,0:T(8,128)(2,1)S(1)}, bf16[4,32,1152]{2,1,0:T(8,128)(2,1)S(1)}, u32[]{:S(2)}, u32[]{:S(2)}) %collective-permute-start.2) | collective-permute-done | bytes 294944 | tf_op jit(solution)/shard_map/ppermute | solution.py:68
  130.2 3.2 collective-permute-start.3
  133.7 0.7 fusion.55
  134.4 12.1 collective-permute-done.3
  146.5 1.2 maximum_select_fusion.2
  147.7 4.8 collective-permute-start.4
  152.5 2.0 maximum_select_fusion.1
  154.6 0.9 convert_convert_fusion.1
  155.5 1.0 fusion.26
  156.6 1.2 shift_right_arithmetic.71
  157.8 0.8 fusion.53
  159.4 18.2 %collective-permute-done.4 = bf16[16,32,1152]{2,1,0:T(8,128)(2,1)} collective-permute-done((bf16[16,32,1152]{2,1,0:T(8,128)(2,1)}, bf16[16,32,1152]{2,1,0:T(8,128)(2,1)}, u32[]{:S(2)}, u32[]{:S(2)}) %collective-permute-start.4) | collective-permute-done | bytes 1179680 | tf_op jit(solution)/shard_map/ppermute | solution.py:68
  177.6 2.6 maximum_select_fusion
  180.7 0.9 copy-done
  182.2 1.7 shift_right_arithmetic.65
  183.9 2.2 fusion.9
  186.1 2.5 subtract_negate_fusion.1
  188.7 1.6 fusion
  190.3 1.5 fusion.1
  191.8 1.7 fusion.2
  193.5 1.6 fusion.3
  195.1 0.6 maximum_bitcast_fusion.2
  195.8 6.0 exponential_convert_fusion.3
  201.8 0.8 fusion.43
  202.6 0.8 fusion.41
  203.3 0.8 fusion.39
  204.1 0.8 fusion.37
  205.0 0.6 gather_fusion
  205.7 22.1 %all_to_all.5 = f32[16,1,128]{2,1,0:T(1,128)S(1)} all-to-all(f32[16,1,128]{2,1,0:T(1,128)S(1)} %reshape.100), channel_id=1, replica_groups=mesh['grp'=16,'dev'=32] {'grp'}, dimensions={0} | all-to-all | bytes 16384 | tf_op jit(solution)/shard_map/all_to_all | solution.py:114
  227.8 0.5 broadcast.108
  228.3 0.7 reduce.3
  229.1 0.6 broadcast_multiply_fusion.1
  229.7 1390.9 %all-gather.4.cloned.1.call-done = f32[512,4,512]{2,1,0:T(4,128)} async-done(((f32[1,4,512]{2,1,0:T(4,128)}), f32[512,4,512]{2,1,0:T(4,128)}) %all-gather.4.cloned.1.call-update) | async-done | bytes 4194320 | tf_op jit(solution)/shard_map/all_gather | solution.py:116
  1620.6 2.8 reduce_sum.115
  1623.9 0.5 rsqrt_multiply_fusion
  (56 shorter events, 4.0 us)
Async XLA Ops:
  7.2 1613.4 %all-gather.4.cloned.1.call-start = ((), (), s32[]{:S(2)}) async-start(), calls=%async_computation.1 | async-start | bytes 4202496 | tf_op jit(solution)/shard_map/all_gather | solution.py:116
  9.7 6.4 collective-permute-start.5
  16.1 10.0 collective-permute-start.6
  22.5 20.1 %collective-permute-start = (bf16[1,32,1152]{2,1,0:T(8,128)(2,1)S(1)}, bf16[1,32,1152]{2,1,0:T(8,128)(2,1)S(1)}, u32[]{:S(2)}, u32[]{:S(2)}) collective-permute-start(bf16[1,32,1152]{2,1,0:T(8,128)(2,1)S(1)} %maximum_bitcast_fusion.1), channel_id=1, source_target_pairs={{0,1},{1,0},{2,3},{3,2},{4,5},{5,4},{6,7},{7,6},{8,9},{9,8},{10,11... | collective-permute-start | bytes 221192 | tf_op jit(solution)/shard_map/ppermute | solution.py:68
  26.2 74.5 %collective-permute-start.7 = (bf16[4,32,2176]{2,1,0:T(8,128)(2,1)S(1)}, bf16[4,32,2176]{2,1,0:T(8,128)(2,1)S(1)}, u32[]{:S(2)}, u32[]{:S(2)}) collective-permute-start(bf16[4,32,2176]{2,1,0:T(8,128)(2,1)S(1)} %maximum_select_fusion.5), channel_id=1, source_target_pairs={{0,256},{32,288},{64,320},{96,352},{128,384},{160,416},{192,448},{... | collective-permute-start | bytes 1671176 | tf_op jit(solution)/shard_map/ppermute | solution.py:68
  42.7 90.8 %copy-start.6 = (f32[16]{0:T(128)S(1)}, f32[16]{0:T(128)}, u32[]{:S(2)}) copy-start(f32[16]{0:T(128)} %param.11) | copy-start | bytes 196
  42.7 90.8 %copy-start.7 = (s32[4]{0:T(128)S(1)}, s32[4]{0:T(128)}, u32[]{:S(2)}) copy-start(s32[4]{0:T(128)} %param.12) | copy-start | bytes 52
  42.7 55.9 %collective-permute-start.1 = (bf16[2,32,1152]{2,1,0:T(8,128)(2,1)S(1)}, bf16[2,32,1152]{2,1,0:T(8,128)(2,1)S(1)}, u32[]{:S(2)}, u32[]{:S(2)}) collective-permute-start(bf16[2,32,1152]{2,1,0:T(8,128)(2,1)S(1)} %maximum_select_fusion.8), channel_id=1, source_target_pairs={{0,2},{1,3},{2,0},{3,1},{4,6},{5,7},{6,4},{7,5},{8,10},{9,11},{10,... | collective-permute-start | bytes 442376 | tf_op jit(solution)/shard_map/ppermute | solution.py:68
  98.6 31.4 %collective-permute-start.2 = (bf16[4,32,1152]{2,1,0:T(8,128)(2,1)S(1)}, bf16[4,32,1152]{2,1,0:T(8,128)(2,1)S(1)}, u32[]{:S(2)}, u32[]{:S(2)}) collective-permute-start(bf16[4,32,1152]{2,1,0:T(8,128)(2,1)S(1)} %maximum_select_fusion.6), channel_id=1, source_target_pairs={{0,4},{1,5},{2,6},{3,7},{4,0},{5,1},{6,2},{7,3},{8,12},{9,13},{10,... | collective-permute-start | bytes 884744 | tf_op jit(solution)/shard_map/ppermute | solution.py:68
  100.9 51.6 %collective-permute-start.8 = (bf16[8,32,2176]{2,1,0:T(8,128)(2,1)S(1)}, bf16[8,32,2176]{2,1,0:T(8,128)(2,1)}, u32[]{:S(2)}, u32[]{:S(2)}) collective-permute-start(bf16[8,32,2176]{2,1,0:T(8,128)(2,1)S(1)} %maximum_select_fusion.3), channel_id=1, source_target_pairs={{0,32},{32,0},{64,96},{96,64},{128,160},{160,128},{192,224},{224,1... | collective-permute-start | bytes 3342344 | tf_op jit(solution)/shard_map/ppermute | solution.py:68
  130.2 16.3 collective-permute-start.3
  147.7 29.9 %collective-permute-start.4 = (bf16[16,32,1152]{2,1,0:T(8,128)(2,1)}, bf16[16,32,1152]{2,1,0:T(8,128)(2,1)}, u32[]{:S(2)}, u32[]{:S(2)}) collective-permute-start(bf16[16,32,1152]{2,1,0:T(8,128)(2,1)} %maximum_select_fusion.2), channel_id=1, source_target_pairs={{0,16},{1,17},{2,18},{3,19},{4,20},{5,21},{6,22},{7,23},{8,24},{9,... | collective-permute-start | bytes 3538952 | tf_op jit(solution)/shard_map/ppermute | solution.py:68
  154.5 4.1 copy-start.2
  157.8 1.3 copy-start.3
  180.2 1.4 copy-start
  183.8 2.3 copy-start.1
  193.5 2.3 copy-start.5
  1623.4 1.0 copy-start.4
Sparse Core Ops, SparseCore 0:
  195.9 1424.6 all-gather.3
